TPU v7x, 512 devices: a whole 4x4x16 slice. The times are simulated.
512 devices in a mesh: smp: 16 (over z), par: 32 (over x, y, core).
Axes of the slice: x: 4, y: 4, z: 16, core: 2. Of those that a mesh axis runs over, the one named last changes fastest.
Arguments:
- jacobian: bfloat16 [4096, 16384], P('smp', 'par'), may hold values from -52 to 52
Outputs:
- panel_factor: float32 [4096, 512], P('smp')
- schur_part: float32 [4096, 4096], P('smp', 'par')
All inputs are finite; a program needn't handle non-finite values.
Results may differ from a plain program's by a relative error of at most 0.0022.
Values may be sent and summed in bfloat16 or wider, within the bound.
No kernel may reach another device: no remote copies, remote signals or barrier semaphores. Data moves between devices by JAX's collectives and lax.ppermute only.
A program may use at most 64 MiB of HBM per device.

v0:
```python
import jax
import jax.numpy as jnp
from jax import lax
from jax.sharding import PartitionSpec as P

PANEL = 512
shift_scale = 0.01


def shards(jacobian):
    row_count, par_width = jacobian.shape
    par_count = lax.axis_size("par")
    smp_count = lax.axis_size("smp")
    sample_total = row_count * smp_count
    param_total = par_width * par_count
    col_width = sample_total // par_count
    row_index = lax.axis_index("smp")
    col_index = lax.axis_index("par")
    widened = jacobian.astype(jnp.float32)
    col_mean = lax.psum(jnp.sum(widened, axis=0), "smp") / sample_total
    centered = (widened - col_mean).astype(jnp.bfloat16)
    gathered = lax.all_gather(centered, "smp", axis=0, tiled=True)
    gram_tile = lax.psum_scatter(
        lax.dot_general(
            gathered, centered, (((1,), (1,)), ((), ())), preferred_element_type=jnp.float32
        )
        / param_total,
        "par",
        scatter_dimension=0,
        tiled=True,
    ).T
    global_rows = row_index * row_count + jnp.arange(row_count, dtype=jnp.int32)
    global_cols = col_index * col_width + jnp.arange(col_width, dtype=jnp.int32)
    diag_mask = global_rows[:, None] == global_cols[None, :]
    trace_total = lax.psum(jnp.sum(jnp.where(diag_mask, gram_tile, 0.0)), ("smp", "par"))
    shift_value = shift_scale * trace_total / sample_total
    shifted = gram_tile + jnp.where(diag_mask, shift_value, 0.0)
    col_keep = (col_index < PANEL // col_width).astype(jnp.float32)
    start_col = jnp.minimum(col_index, PANEL // col_width - 1) * col_width
    placed_rows = lax.dynamic_update_slice(
        jnp.zeros((row_count, PANEL), jnp.float32), shifted * col_keep, (jnp.int32(0), start_col)
    )
    panel_rows = lax.psum(placed_rows, "par")
    row_keep = (row_index < PANEL // row_count).astype(jnp.float32)
    start_row = jnp.minimum(row_index, PANEL // row_count - 1) * row_count
    top_square = lax.dynamic_update_slice(
        jnp.zeros((PANEL, PANEL), jnp.float32), panel_rows * row_keep, (start_row, jnp.int32(0))
    )
    top_band = lax.dynamic_update_slice(
        jnp.zeros((PANEL, col_width), jnp.float32), shifted * row_keep, (start_row, jnp.int32(0))
    )
    square, band_rows = lax.psum((top_square, top_band), "smp")
    factor = jnp.linalg.cholesky(square)
    panel_out = jax.scipy.linalg.solve_triangular(factor, panel_rows.T, lower=True).T
    band_factor = jax.scipy.linalg.solve_triangular(factor, band_rows, lower=True)
    schur_tile = shifted - jnp.dot(panel_out, band_factor, precision=lax.Precision.HIGHEST)
    return (panel_out, schur_tile)


def solution(mesh):
    placed = (P("smp", "par"),)
    return jax.shard_map(
        shards,
        mesh=mesh,
        in_specs=placed,
        out_specs=(P("smp", None), P("smp", "par")),
        check_vma=False,
    )
```

profile of v0, /device:TPU:2, one launch (start us, length us, event | category | flops | bytes accessed | tf_op | source)
XLA Modules:
  0.0 757.3 jit_solution(15600301314958486580)
XLA Ops:
  7.2 1.0 convert_reduce_fusion
  8.2 36.5 %psum.35 = f32[512]{0:T(512)S(1)} all-reduce(f32[512]{0:T(512)S(1)} %convert_reduce_fusion), channel_id=1, replica_groups=mesh['smp'=16,'par'=32] {'smp'}, use_global_device_ids=true, to_apply=%region_1.0 | all-reduce | flops 512 | bytes 4096 | tf_op jit(solution)/shard_map/psum | solution.py:20
  44.7 1.7 fusion.1
  46.5 74.9 %all-gather.2.cloned.1.call-done = bf16[4096,512]{1,0:T(8,128)(2,1)} async-done(((bf16[256,512]{1,0:T(8,128)(2,1)}), bf16[4096,512]{1,0:T(8,128)(2,1)}) %all-gather.2.cloned.1.call-update) | async-done | bytes 4194320 | tf_op jit(solution)/shard_map/all_gather | solution.py:22
  121.4 5.4 convolution_multiply_fusion
  126.9 101.3 %reduce-scatter.2.cloned.1.call-done = f32[128,256]{1,0:T(8,128)} async-done(((f32[4096,256]{1,0:T(8,128)}), f32[128,256]{1,0:T(8,128)}) %reduce-scatter.2.cloned.1.call-update) | async-done | bytes 131088 | tf_op jit(solution)/shard_map/reduce_scatter | solution.py:23
  228.2 1.6 fusion.29
  229.8 101.8 %psum.36 = f32[]{:T(128)} all-reduce(f32[]{:T(128)} %fusion.29), channel_id=1, replica_groups=mesh['smp'=16,'par'=32] {'smp','par'}, use_global_device_ids=true, to_apply=%region_4.5 | all-reduce | flops 1 | bytes 8 | tf_op jit(solution)/shard_map/psum | solution.py:35
  332.3 1.0 multiply_dynamic-update-slice_fusion.1
  333.4 0.8 copy-done.2
  334.4 130.4 %all-reduce.5.cloned.1.call-done = f32[256,512]{0,1:T(8,128)} async-done(((f32[256,512]{0,1:T(8,128)}), f32[256,512]{0,1:T(8,128)}) %all-reduce.5.cloned.1.call-update) | async-done | bytes 524304 | tf_op jit(solution)/shard_map/psum | solution.py:43
  464.9 1.1 multiply_dynamic-update-slice_fusion
  466.0 1.0 copy-done
  467.1 140.6 %all-reduce.7.cloned.1.call-done = (f32[512,512]{0,1:T(8,128)}, f32[512,128]{0,1:T(8,128)}) async-done(((f32[512,512]{0,1:T(8,128)}, f32[512,128]{0,1:T(8,128)}), (f32[512,512]{0,1:T(8,128)}, f32[512,128]{0,1:T(8,128)})) %all-reduce.7.cloned.1.call-update) | async-done | bytes 1310736 | tf_op jit(solution)/shard_map/psum | solution.py:52
  607.7 1.6 copy.3
  609.3 1.4 fusion
  610.7 11.7 %cholesky.103 = f32[128,128]{1,0:T(8,128)S(1)} custom-call(f32[128,128]{1,0:T(8,128)S(1)} %cholesky.263), custom_call_target="Cholesky" | custom-call | tf_op jit(solution)/shard_map/jit(cholesky)/cholesky | solution.py:53
  622.5 9.8 %custom-call.34 = f32[1,128,128]{1,2,0:T(8,128)S(1)} custom-call(f32[1,128,128]{2,1,0:T(8,128)S(1)} %get-tuple-element.35), custom_call_target="InvertDiagBlocksLowerTriangular" | custom-call | tf_op jit(solution)/shard_map/jit(cholesky)/cholesky | solution.py:53
  633.0 11.7 %cholesky.215 = f32[128,128]{1,0:T(8,128)S(1)} custom-call(f32[128,128]{1,0:T(8,128)S(1)} %cholesky.267), custom_call_target="Cholesky" | custom-call | tf_op jit(solution)/shard_map/jit(cholesky)/cholesky | solution.py:53
  645.2 10.0 %custom-call.35 = f32[1,128,128]{1,2,0:T(8,128)S(1)} custom-call(f32[1,128,128]{2,1,0:T(8,128)S(1)} %get-tuple-element.33), custom_call_target="InvertDiagBlocksLowerTriangular" | custom-call | tf_op jit(solution)/shard_map/jit(cholesky)/cholesky | solution.py:53
  656.2 11.7 %cholesky.236 = f32[128,128]{1,0:T(8,128)S(1)} custom-call(f32[128,128]{1,0:T(8,128)S(1)} %cholesky.272), custom_call_target="Cholesky" | custom-call | tf_op jit(solution)/shard_map/jit(cholesky)/cholesky | solution.py:53
  668.0 9.8 %custom-call.36 = f32[1,128,128]{1,2,0:T(8,128)S(1)} custom-call(f32[1,128,128]{2,1,0:T(8,128)S(1)} %get-tuple-element.31), custom_call_target="InvertDiagBlocksLowerTriangular" | custom-call | tf_op jit(solution)/shard_map/jit(cholesky)/cholesky | solution.py:53
  678.6 11.9 %cholesky.253 = f32[128,128]{1,0:T(8,128)S(1)} custom-call(f32[128,128]{1,0:T(8,128)S(1)} %convolution_subtract_fusion.9), custom_call_target="Cholesky" | custom-call | tf_op jit(solution)/shard_map/jit(cholesky)/cholesky | solution.py:53
  690.7 0.7 compare_reduce_fusion.1
  695.4 8.8 %while.1 = (s32[]{:T(128)}, f32[512,512]{0,1:T(8,128)S(1)}, s32[4,2]{0,1:T(2,128)S(1)}, f32[4,128,128]{2,1,0:T(8,128)S(1)}, s32[]{:T(128)}) while((s32[]{:T(128)}, f32[512,512]{0,1:T(8,128)S(1)}, s32[4,2]{0,1:T(2,128)S(1)}, f32[4,128,128]{2,1,0:T(8,128)S(1)}, s32[]{:T(128)}) %tuple.30), condition=%wide.while_cond, body=%wide.while_body.sunk | while | flops 2 | bytes 393321 | solution.py:54
  696.1 1.4 dynamic-slice.7
  698.3 1.4 dynamic-slice.7
  700.5 1.4 dynamic-slice.7
  702.6 1.4 dynamic-slice.7
  704.2 39.3 %custom-call.37 = f32[4,128,128]{1,2,0:T(8,128)S(1)} custom-call(f32[4,128,128]{2,1,0:T(8,128)S(1)} %get-tuple-element.9), custom_call_target="InvertDiagBlocksLowerTriangular" | custom-call | tf_op jit(solution)/shard_map/jit(_solve_triangular)/triangular_solve | solution.py:54
  749.0 0.8 copy.14
  749.8 1.0 copy.13
  (85 shorter events, 13.6 us)
Async XLA Ops:
  7.2 114.2 %all-gather.2.cloned.1.call-start = ((), (), s32[]{:S(2)}) async-start(), calls=%async_computation.1 | async-start | bytes 4456448 | tf_op jit(solution)/shard_map/all_gather | solution.py:22
  46.5 181.7 %reduce-scatter.2.cloned.1.call-start = ((), (), s32[]{:S(2)}) async-start(), calls=%async_computation.2 | async-start | bytes 4325376 | tf_op jit(solution)/shard_map/reduce_scatter | solution.py:23
  126.8 337.9 %all-reduce.5.cloned.1.call-start = ((), (), s32[]{:S(2)}) async-start(), calls=%async_computation.3 | async-start | bytes 1048576 | tf_op jit(solution)/shard_map/psum | solution.py:43
  333.3 0.8 copy-start.2
  333.4 132.6 %copy-start.3 = (f32[512,128]{0,1:T(8,128)}, f32[512,128]{0,1:T(8,128)S(1)}, u32[]{:S(2)}) copy-start(f32[512,128]{0,1:T(8,128)S(1)} %get-tuple-element.28) | copy-start | bytes 786436
  334.2 273.6 %all-reduce.7.cloned.1.call-start = ((), (), s32[]{:S(2)}) async-start(), calls=%async_computation.4 | async-start | bytes 2621440 | tf_op jit(solution)/shard_map/psum | solution.py:52
  466.0 1.0 copy-start
  645.0 98.5 %copy-start.5 = (f32[512,128]{0,1:T(8,128)S(1)}, f32[512,128]{0,1:T(8,128)}, u32[]{:S(2)}) copy-start(f32[512,128]{0,1:T(8,128)} %get-tuple-element.25) | copy-start | bytes 786436
  655.6 90.3 %copy-start.1 = (f32[256,512]{0,1:T(8,128)S(1)}, f32[256,512]{0,1:T(8,128)}, u32[]{:S(2)}) copy-start(f32[256,512]{0,1:T(8,128)} %all-reduce.5.cloned.1.call-done) | copy-start | bytes 1572868
  695.4 53.0 %copy-start.4 = (f32[128,256]{1,0:T(8,128)S(1)}, f32[128,256]{1,0:T(8,128)}, u32[]{:S(2)}) copy-start(f32[128,256]{1,0:T(8,128)} %reduce-scatter.2.cloned.1.call-done) | copy-start | bytes 393220
Sparse Core Ops, SparseCore 0:
  46.6 74.7 all-gather.1
  126.9 101.1 reduce-scatter.1
  334.3 130.4 all-reduce.4
  467.2 140.4 all-reduce.6
where the time goes:
time: 758 us; the launch traced here: 757 us
  waiting for transfers between devices  447 us (59%)
  blocking collectives  138 us (18%)
  other arithmetic  126 us (17%)
  between operations  17.4 us (2%)
  local copies, waits for them, and re-layouts  14.6 us (2%)
  matrix products  13.1 us (2%)
    psum x1, waiting for transfers between devices, shards(): square, band_rows = lax.psum((top_square, top_band), 'smp')  141 us
    psum x1, waiting for transfers between devices, shards(): panel_rows = lax.psum(placed_rows, 'par')  130 us
    psum x1, blocking collectives, shards(): lax.psum(jnp.sum(jnp.where(diag_mask, gram_tile, 0.0)), ('smp', 'par'))  102 us
    reduce_scatter x1, waiting for transfers between devices, shards(): lax.psum_scatter(lax.dot_general(gathered, centered, (((1,), (1,)), ((),...  101 us
    another operation x14, other arithmetic, shards(): factor = jnp.linalg.cholesky(square)  78.8 us
    all_gather x1, waiting for transfers between devices, shards(): gathered = lax.all_gather(centered, 'smp', axis=0, tiled=True)  74.9 us
    another operation x3, other arithmetic, shards(): jax.scipy.linalg.solve_triangular(factor, panel_rows.T, lower=True)  39.4 us
    psum x1, blocking collectives, shards(): col_mean = lax.psum(jnp.sum(widened, axis=0), 'smp') / sample_total  36.5 us
  transfers between devices with their start and end apart: 4, of which 4 were waited for; matrix products, arithmetic and copies ran while one was open for 0% of the time, Pallas kernels for 0%

commit v1 on v0

--- a/solution.py
+++ b/solution.py
@@ -19,7 +19,11 @@
     widened = jacobian.astype(jnp.float32)
     col_mean = lax.psum(jnp.sum(widened, axis=0), "smp") / sample_total
     centered = (widened - col_mean).astype(jnp.bfloat16)
-    gathered = lax.all_gather(centered, "smp", axis=0, tiled=True)
+    length = lax.axis_size("smp")
+    repeats = [length if d == 0 else 1 for d in range(centered.ndim)]
+    gathered = lax.all_to_all(
+        jnp.tile(centered, repeats), "smp", split_axis=0, concat_axis=0, tiled=True
+    )
     gram_tile = lax.psum_scatter(
         lax.dot_general(
             gathered, centered, (((1,), (1,)), ((), ())), preferred_element_type=jnp.float32

time: 758 us -> 865 us (1.14)
  blocking collectives: 138 us -> 324 us
  waiting for transfers between devices: 447 us -> 372 us
    all_to_all x0 -> x1, blocking collectives: none -> 185 us  [shards(): lax.all_to_all(jnp.tile(centered, repeats), 'smp', split_axis=0, concat_a...]
    all_gather x1 -> x0, waiting for transfers between devices: 74.9 us -> none  [shards(): gathered = lax.all_gather(centered, 'smp', axis=0, tiled=True)]
  transfers between devices with their start and end apart: 4 -> 3, of which waited for: 4 -> 3; matrix products, arithmetic and copies ran while one was open for 0% -> 0% of each run, Pallas kernels for 0% -> 0%
where the time goes in v1:
time: 865 us
  waiting for transfers between devices  372 us (43%)
  blocking collectives  324 us (37%)
  other arithmetic  126 us (15%)
  between operations  17.4 us (2%)
  local copies, waits for them, and re-layouts  15 us (2%)
  matrix products  10.9 us (1%)
    all_to_all x1, blocking collectives, shards(): lax.all_to_all(jnp.tile(centered, repeats), 'smp', split_axis=0, concat_a...  185 us
    psum x1, waiting for transfers between devices, shards(): square, band_rows = lax.psum((top_square, top_band), 'smp')  141 us
    psum x1, waiting for transfers between devices, shards(): panel_rows = lax.psum(placed_rows, 'par')  130 us
    psum x1, blocking collectives, shards(): lax.psum(jnp.sum(jnp.where(diag_mask, gram_tile, 0.0)), ('smp', 'par'))  102 us
    reduce_scatter x1, waiting for transfers between devices, shards(): lax.psum_scatter(lax.dot_general(gathered, centered, (((1,), (1,)), ((),...  101 us
    another operation x14, other arithmetic, shards(): factor = jnp.linalg.cholesky(square)  78.8 us
    another operation x3, other arithmetic, shards(): jax.scipy.linalg.solve_triangular(factor, panel_rows.T, lower=True)  39.4 us
    psum x1, blocking collectives, shards(): col_mean = lax.psum(jnp.sum(widened, axis=0), 'smp') / sample_total  36.5 us
  transfers between devices with their start and end apart: 3, of which 3 were waited for; matrix products, arithmetic and copies ran while one was open for 0% of the time, Pallas kernels for 0%

profile of v1, /device:TPU:2, one launch (start us, length us, event | category | flops | bytes accessed | tf_op | source)
XLA Modules:
  0.0 864.8 jit_solution(3920713979308305435)
XLA Ops:
  7.2 1.0 convert_reduce_fusion
  8.2 36.5 %psum.35 = f32[512]{0:T(512)S(1)} all-reduce(f32[512]{0:T(512)S(1)} %convert_reduce_fusion), channel_id=1, replica_groups=mesh['smp'=16,'par'=32] {'smp'}, use_global_device_ids=true, to_apply=%region_1.0 | all-reduce | flops 512 | bytes 4096 | tf_op jit(solution)/shard_map/psum | solution.py:20
  44.7 1.0 fusion.1
  46.1 185.3 %all_to_all.9 = bf16[16,256,512]{2,1,0:T(8,128)(2,1)S(1)} all-to-all(bf16[16,256,512]{2,1,0:T(8,128)(2,1)S(1)} %tile.2), channel_id=1, replica_groups=mesh['smp'=16,'par'=32] {'smp'}, dimensions={0} | all-to-all | bytes 8388608 | tf_op jit(solution)/shard_map/all_to_all | solution.py:24
  231.4 3.2 convolution_multiply_fusion
  234.8 100.9 %reduce-scatter.2.cloned.1.call-done = f32[128,256]{1,0:T(8,128)} async-done(((f32[4096,256]{1,0:T(8,128)}), f32[128,256]{1,0:T(8,128)}) %reduce-scatter.2.cloned.1.call-update) | async-done | bytes 131088 | tf_op jit(solution)/shard_map/reduce_scatter | solution.py:27
  335.7 1.6 fusion.29
  337.3 101.8 %psum.36 = f32[]{:T(128)} all-reduce(f32[]{:T(128)} %fusion.29), channel_id=1, replica_groups=mesh['smp'=16,'par'=32] {'smp','par'}, use_global_device_ids=true, to_apply=%region_4.5 | all-reduce | flops 1 | bytes 8 | tf_op jit(solution)/shard_map/psum | solution.py:39
  439.9 1.0 multiply_dynamic-update-slice_fusion.1
  440.9 0.8 copy-done.2
  441.9 130.3 %all-reduce.5.cloned.1.call-done = f32[256,512]{0,1:T(8,128)} async-done(((f32[256,512]{0,1:T(8,128)}), f32[256,512]{0,1:T(8,128)}) %all-reduce.5.cloned.1.call-update) | async-done | bytes 524304 | tf_op jit(solution)/shard_map/psum | solution.py:47
  572.4 1.1 multiply_dynamic-update-slice_fusion
  573.5 1.0 copy-done
  574.6 140.7 %all-reduce.7.cloned.1.call-done = (f32[512,512]{0,1:T(8,128)}, f32[512,128]{0,1:T(8,128)}) async-done(((f32[512,512]{0,1:T(8,128)}, f32[512,128]{0,1:T(8,128)}), (f32[512,512]{0,1:T(8,128)}, f32[512,128]{0,1:T(8,128)})) %all-reduce.7.cloned.1.call-update) | async-done | bytes 1310736 | tf_op jit(solution)/shard_map/psum | solution.py:56
  715.2 1.6 copy.3
  716.8 1.4 fusion
  718.3 11.7 %cholesky.103 = f32[128,128]{1,0:T(8,128)S(1)} custom-call(f32[128,128]{1,0:T(8,128)S(1)} %cholesky.263), custom_call_target="Cholesky" | custom-call | tf_op jit(solution)/shard_map/jit(cholesky)/cholesky | solution.py:57
  730.0 9.8 %custom-call.34 = f32[1,128,128]{1,2,0:T(8,128)S(1)} custom-call(f32[1,128,128]{2,1,0:T(8,128)S(1)} %get-tuple-element.35), custom_call_target="InvertDiagBlocksLowerTriangular" | custom-call | tf_op jit(solution)/shard_map/jit(cholesky)/cholesky | solution.py:57
  740.5 11.7 %cholesky.215 = f32[128,128]{1,0:T(8,128)S(1)} custom-call(f32[128,128]{1,0:T(8,128)S(1)} %cholesky.267), custom_call_target="Cholesky" | custom-call | tf_op jit(solution)/shard_map/jit(cholesky)/cholesky | solution.py:57
  752.7 10.0 %custom-call.35 = f32[1,128,128]{1,2,0:T(8,128)S(1)} custom-call(f32[1,128,128]{2,1,0:T(8,128)S(1)} %get-tuple-element.33), custom_call_target="InvertDiagBlocksLowerTriangular" | custom-call | tf_op jit(solution)/shard_map/jit(cholesky)/cholesky | solution.py:57
  763.7 11.7 %cholesky.236 = f32[128,128]{1,0:T(8,128)S(1)} custom-call(f32[128,128]{1,0:T(8,128)S(1)} %cholesky.272), custom_call_target="Cholesky" | custom-call | tf_op jit(solution)/shard_map/jit(cholesky)/cholesky | solution.py:57
  775.6 9.8 %custom-call.36 = f32[1,128,128]{1,2,0:T(8,128)S(1)} custom-call(f32[1,128,128]{2,1,0:T(8,128)S(1)} %get-tuple-element.31), custom_call_target="InvertDiagBlocksLowerTriangular" | custom-call | tf_op jit(solution)/shard_map/jit(cholesky)/cholesky | solution.py:57
  786.2 11.9 %cholesky.253 = f32[128,128]{1,0:T(8,128)S(1)} custom-call(f32[128,128]{1,0:T(8,128)S(1)} %convolution_subtract_fusion.9), custom_call_target="Cholesky" | custom-call | tf_op jit(solution)/shard_map/jit(cholesky)/cholesky | solution.py:57
  798.2 0.7 compare_reduce_fusion.1
  802.9 8.8 %while.1 = (s32[]{:T(128)}, f32[512,512]{0,1:T(8,128)S(1)}, s32[4,2]{0,1:T(2,128)S(1)}, f32[4,128,128]{2,1,0:T(8,128)S(1)}, s32[]{:T(128)}) while((s32[]{:T(128)}, f32[512,512]{0,1:T(8,128)S(1)}, s32[4,2]{0,1:T(2,128)S(1)}, f32[4,128,128]{2,1,0:T(8,128)S(1)}, s32[]{:T(128)}) %tuple.30), condition=%wide.while_cond, body=%wide.while_body.sunk | while | flops 2 | bytes 393321 | solution.py:58
  803.6 1.4 dynamic-slice.7
  805.8 1.4 dynamic-slice.7
  808.0 1.4 dynamic-slice.7
  810.2 1.4 dynamic-slice.7
  811.7 39.3 %custom-call.37 = f32[4,128,128]{1,2,0:T(8,128)S(1)} custom-call(f32[4,128,128]{2,1,0:T(8,128)S(1)} %get-tuple-element.9), custom_call_target="InvertDiagBlocksLowerTriangular" | custom-call | tf_op jit(solution)/shard_map/jit(_solve_triangular)/triangular_solve | solution.py:58
  856.6 0.8 copy.14
  857.3 1.0 copy.13
  (84 shorter events, 14.0 us)
Async XLA Ops:
  7.2 328.5 %reduce-scatter.2.cloned.1.call-start = ((), (), s32[]{:S(2)}) async-start(), calls=%async_computation.2 | async-start | bytes 4325376 | tf_op jit(solution)/shard_map/reduce_scatter | solution.py:27
  234.7 337.6 %all-reduce.5.cloned.1.call-start = ((), (), s32[]{:S(2)}) async-start(), calls=%async_computation.3 | async-start | bytes 1048576 | tf_op jit(solution)/shard_map/psum | solution.py:47
  440.9 0.8 copy-start.2
  440.9 132.6 %copy-start.3 = (f32[512,128]{0,1:T(8,128)}, f32[512,128]{0,1:T(8,128)S(1)}, u32[]{:S(2)}) copy-start(f32[512,128]{0,1:T(8,128)S(1)} %get-tuple-element.28) | copy-start | bytes 786436
  441.7 273.5 %all-reduce.7.cloned.1.call-start = ((), (), s32[]{:S(2)}) async-start(), calls=%async_computation.4 | async-start | bytes 2621440 | tf_op jit(solution)/shard_map/psum | solution.py:56
  573.5 1.0 copy-start
  752.5 98.6 %copy-start.5 = (f32[512,128]{0,1:T(8,128)S(1)}, f32[512,128]{0,1:T(8,128)}, u32[]{:S(2)}) copy-start(f32[512,128]{0,1:T(8,128)} %get-tuple-element.25) | copy-start | bytes 786436
  763.1 90.3 %copy-start.1 = (f32[256,512]{0,1:T(8,128)S(1)}, f32[256,512]{0,1:T(8,128)}, u32[]{:S(2)}) copy-start(f32[256,512]{0,1:T(8,128)} %all-reduce.5.cloned.1.call-done) | copy-start | bytes 1572868
  802.9 53.0 %copy-start.4 = (f32[128,256]{1,0:T(8,128)S(1)}, f32[128,256]{1,0:T(8,128)}, u32[]{:S(2)}) copy-start(f32[128,256]{1,0:T(8,128)} %reduce-scatter.2.cloned.1.call-done) | copy-start | bytes 393220
Sparse Core Ops, SparseCore 0:
  234.8 100.8 reduce-scatter.1
  441.8 130.3 all-reduce.4
  574.7 140.5 all-reduce.6
